TPU v7x, 512 devices: a whole 4x8x8 slice. The times are simulated.
512 devices in a mesh: row: 64 (over z_hi, y, x), col: 8 (over z_lo, core).
Axes of the slice: x: 4, y: 8, z: 8 (z_hi: 2, z_lo: 4; z = z_hi * 4 + z_lo), core: 2. Of those that a mesh axis runs over, the one named last changes fastest.
Arguments:
- queries: bfloat16 [64, 1024, 768], P('row', 'col'), may hold values from -20 to 20
- key_vectors: bfloat16 [64, 1024, 768], P('row', 'col'), may hold values from -20 to 20
- value_vectors: bfloat16 [64, 1024, 768], P('row', 'col'), may hold values from -6 to 6
- cotangent: bfloat16 [64, 1024, 768], P('row', 'col'), may hold values from -6 to 6
Outputs:
- attended: bfloat16 [64, 1024, 768], P('row', 'col')
- query_grad: bfloat16 [64, 1024, 768], P('row', 'col')
- key_grad: bfloat16 [64, 1024, 768], P('row', 'col')
- value_grad: bfloat16 [64, 1024, 768], P('row', 'col')
- logit_peak: float32 [12], replicated
All inputs are finite; a program needn't handle non-finite values.
Results may differ from a plain program's by a relative error of at most 0.023.
Values may be sent and summed in bfloat16 or wider, within the bound.
No kernel may reach another device: no remote copies, remote signals or barrier semaphores. Data moves between devices by JAX's collectives and lax.ppermute only.
A program may use at most 128 MiB of HBM per device.

v0:
```python
import jax
import jax.numpy as jnp
from jax import lax
from jax.sharding import PartitionSpec as P
from jax.experimental import pallas as pl
from jax.experimental.pallas import tpu as pltpu

H = 12
HD = 64
DILATION_STEP = 16
HALF_EXTENT = 3


big_negative = -1e30


def passed_along(value, axis, steps):
    count = lax.axis_size(axis)
    first, last = (max(0, -steps), min(count, count - steps))
    return lax.ppermute(value, axis, [(source, source + steps) for source in range(first, last)])


def all_max(value, axes):
    for axis in axes:
        count = lax.axis_size(axis)
        if count & (count - 1):
            value = lax.pmax(value, axis)
            continue
        stride = 1
        while stride < count:
            partner = lax.ppermute(value, axis, [(i, i ^ stride) for i in range(count)])
            value = jnp.maximum(value, partner)
            stride *= 2
    return value


def extended(cells, sides, width):
    for axis, dim in sides:
        count = lax.axis_size(axis)
        ends = count - 1
        head = lax.slice_in_dim(cells, 0, width, axis=dim)
        tail = lax.slice_in_dim(cells, cells.shape[dim] - width, cells.shape[dim], axis=dim)
        cells = jnp.concatenate(
            [
                lax.ppermute(tail, axis, [(i, (i + 1) % count) for i in range(ends)]),
                cells,
                lax.ppermute(head, axis, [((i + 1) % count, i) for i in range(ends)]),
            ],
            axis=dim,
        )
    return cells


def spread_pairs(widened, step_length):
    blocks = {0: widened}
    for row_shift in range(-HALF_EXTENT, HALF_EXTENT + 1):
        if row_shift != 0:
            blocks[row_shift] = passed_along(widened, "row", -row_shift * step_length)
    return jnp.stack([blocks[row_shift] for row_shift in range(-HALF_EXTENT, HALF_EXTENT + 1)])


def return_rows(spill, step_length):
    limit = lax.axis_size("row")
    gathered = spill[HALF_EXTENT]
    for row_shift in range(-HALF_EXTENT, HALF_EXTENT + 1):
        if row_shift != 0 and abs(row_shift) * step_length < limit:
            gathered = gathered + passed_along(
                spill[row_shift + HALF_EXTENT].astype(jnp.bfloat16), "row", row_shift * step_length
            ).astype(jnp.float32)
    return gathered


def head_sums(product, indicator):
    return jnp.einsum("itf,fh->iht", product, indicator, precision=lax.Precision.HIGHEST)


def to_features(per_head):
    return jnp.repeat(jnp.swapaxes(per_head, -1, -2), HD, axis=-1)


LANES = 128


def neighbourhood_body(q_ref, c_ref, kv_ref, mask_ref, att_ref, qg_ref, spill_ref, peak_ref, s_scr):
    f32, bf16 = jnp.float32, jnp.bfloat16
    token_count, feature_count = q_ref.shape
    window = 2 * HALF_EXTENT + 1
    logit_scale = HD ** (-0.5)
    ind = (
        lax.broadcasted_iota(jnp.int32, (feature_count, LANES), 0) // HD
        == lax.broadcasted_iota(jnp.int32, (feature_count, LANES), 1)
    ).astype(bf16)
    ind_t = (
        lax.broadcasted_iota(jnp.int32, (LANES, feature_count), 1) // HD
        == lax.broadcasted_iota(jnp.int32, (LANES, feature_count), 0)
    ).astype(bf16)

    def mm(x, y):
        return jnp.dot(x, y, preferred_element_type=f32)

    def exact_sum(p):
        hi = p.astype(bf16)
        lo = (p - hi.astype(f32)).astype(bf16)
        return mm(hi, ind) + mm(lo, ind)

    def full_sum(p):
        hi = p.astype(bf16)
        r1 = p - hi.astype(f32)
        mid = r1.astype(bf16)
        lo = (r1 - mid.astype(f32)).astype(bf16)
        return mm(hi, ind) + mm(mid, ind) + mm(lo, ind)

    def spread(w):
        return mm(w, ind_t)

    def keys(a, b):
        return kv_ref[a, pl.ds(b * DILATION_STEP, token_count), pl.ds(0, feature_count)].astype(f32)

    def values(a, b):
        return kv_ref[a, pl.ds(b * DILATION_STEP, token_count), pl.ds(feature_count, feature_count)].astype(f32)

    q = q_ref[...].astype(f32)
    c = c_ref[...].astype(f32)
    top = jnp.full((token_count, LANES), big_negative, f32)
    for a in range(window):
        for b in range(window):
            s = exact_sum(q * keys(a, b)) * logit_scale
            s = jnp.where(mask_ref[a * window + b] > 0, s, big_negative)
            s_scr[a * window + b] = s
            top = jnp.maximum(top, s)
    peak_ref[...] = jnp.max(top, axis=0, keepdims=True)
    total = jnp.zeros((token_count, LANES), f32)
    for ab in range(window * window):
        e = jnp.where(mask_ref[ab] > 0, jnp.exp(s_scr[ab] - top), 0.0)
        s_scr[ab] = e
        total = total + e
    att = jnp.zeros((token_count, feature_count), f32)
    for a in range(window):
        for b in range(window):
            w_b = (s_scr[a * window + b] / total).astype(bf16)
            att = att + spread(w_b) * values(a, b)
    att_ref[...] = att.astype(att_ref.dtype)
    drive = full_sum(c * att)
    spill_ref[...] = jnp.zeros(spill_ref.shape, f32)
    qg = jnp.zeros((token_count, feature_count), f32)
    for a in range(window):
        for b in range(window):
            w = s_scr[a * window + b] / total
            v = values(a, b)
            through = exact_sum(c * v)
            slope = spread((w * (through - drive)).astype(bf16))
            qg = qg + slope * keys(a, b)
            rows = pl.ds(b * DILATION_STEP, token_count)
            spill_ref[a, rows, pl.ds(0, feature_count)] += slope * q * logit_scale
            spill_ref[a, rows, pl.ds(feature_count, feature_count)] += spread(w.astype(bf16)) * c
    qg_ref[...] = (qg * logit_scale).astype(qg_ref.dtype)


def neighbourhood_kernel(q, c, kv, mask, interpret=False):
    token_count, feature_count = q.shape
    window = kv.shape[0]
    vmem = pltpu.MemorySpace.VMEM if hasattr(pltpu, "MemorySpace") else pltpu.TPUMemorySpace.VMEM
    spec = pl.BlockSpec(memory_space=vmem)
    return pl.pallas_call(
        neighbourhood_body,
        out_shape=(
            jax.ShapeDtypeStruct((token_count, feature_count), jnp.bfloat16),
            jax.ShapeDtypeStruct((token_count, feature_count), jnp.bfloat16),
            jax.ShapeDtypeStruct(kv.shape, jnp.float32),
            jax.ShapeDtypeStruct((1, LANES), jnp.float32),
        ),
        in_specs=[spec] * 4,
        out_specs=(spec,) * 4,
        scratch_shapes=[pltpu.VMEM((window * window, token_count, LANES), jnp.float32)],
        compiler_params=pltpu.CompilerParams(vmem_limit_bytes=56 * 1024 * 1024),
        interpret=interpret,
    )(q, c, kv, mask)


def on_device(queries, key_vectors, value_vectors, cotangent):
    rows_per_shard, cols_dev, feature_count = queries.shape
    token_count = rows_per_shard * cols_dev
    neighbour_cells = HALF_EXTENT * DILATION_STEP
    step_length = DILATION_STEP // rows_per_shard
    window = 2 * HALF_EXTENT + 1
    logit_scale = HD ** (-0.5)
    row_total = rows_per_shard * lax.axis_size("row")
    col_total = cols_dev * lax.axis_size("col")
    row_place = lax.axis_index("row") * rows_per_shard + jnp.arange(rows_per_shard, dtype=jnp.int32)
    col_place = lax.axis_index("col") * cols_dev + jnp.arange(cols_dev, dtype=jnp.int32)
    shift_list = jnp.arange(-HALF_EXTENT, HALF_EXTENT + 1, dtype=jnp.int32) * DILATION_STEP
    row_target = row_place[None, :] + shift_list[:, None]
    col_target = col_place[None, :] + shift_list[:, None]
    row_usable = (row_target >= 0) & (row_target < row_total)
    col_usable = (col_target >= 0) & (col_target < col_total)
    usable = col_usable[:, None, None, :] & row_usable[None, :, :, None]
    pairs_in = jnp.concatenate([key_vectors, value_vectors], axis=-1)
    widened = extended(pairs_in, (("col", 1),), neighbour_cells)
    stacked = spread_pairs(widened, step_length)

    tokens = lax.broadcasted_iota(jnp.int32, (window * window, token_count, LANES), 2) < H
    usable_ab = jnp.transpose(usable[:, :, 0, :], (1, 0, 2)).reshape(window * window, token_count)
    mask = jnp.where(tokens, usable_ab[..., None], True).astype(jnp.float32)
    attended, query_grad, spill, peak = neighbourhood_kernel(
        queries.reshape(token_count, feature_count),
        cotangent.reshape(token_count, feature_count),
        stacked.reshape(window, cols_dev + 2 * neighbour_cells, 2 * feature_count),
        mask,
    )
    attended = attended.reshape(rows_per_shard, cols_dev, feature_count)
    query_grad = query_grad.reshape(rows_per_shard, cols_dev, feature_count)
    logit_peak = all_max(peak[0, :H], ("col", "row"))
    spill = spill.reshape(window, rows_per_shard, cols_dev + 2 * neighbour_cells, 2 * feature_count)
    gathered = return_rows(spill, step_length)
    west_part = gathered[:, :neighbour_cells]
    east_part = gathered[:, neighbour_cells + cols_dev :]
    owned = gathered[:, neighbour_cells : neighbour_cells + cols_dev]
    from_east = passed_along(west_part.astype(jnp.bfloat16), "col", -1).astype(west_part.dtype)
    from_west = passed_along(east_part.astype(jnp.bfloat16), "col", 1).astype(east_part.dtype)
    owned = owned.at[:, cols_dev - neighbour_cells :].add(from_east)
    owned = owned.at[:, :neighbour_cells].add(from_west)
    key_grad = owned[..., :feature_count].astype(jnp.bfloat16)
    value_grad = owned[..., feature_count:].astype(jnp.bfloat16)
    return (attended, query_grad, key_grad, value_grad, logit_peak)


def solution(mesh):
    placed = (
        P("row", "col", None),
        P("row", "col", None),
        P("row", "col", None),
        P("row", "col", None),
    )
    return jax.shard_map(
        on_device,
        mesh=mesh,
        in_specs=placed,
        out_specs=(
            P("row", "col", None),
            P("row", "col", None),
            P("row", "col", None),
            P("row", "col", None),
            P(),
        ),
        check_vma=False,
    )
```

profile of v0, /device:TPU:1, one launch (start us, length us, event | category | flops | bytes accessed | tf_op | source)
XLA Modules:
  0.0 328.9 jit_solution(5701356814211454763)
XLA Ops:
  0.6 0.9 constant_dynamic-update-slice_fusion.1
  1.6 0.9 constant_dynamic-update-slice_fusion
  2.5 5.4 %collective-permute-start = (bf16[1,48,1536]{2,1,0:T(8,128)(2,1)S(1)}, bf16[1,48,1536]{2,1,0:T(8,128)(2,1)S(1)}, u32[]{:S(2)}, u32[]{:S(2)}) collective-permute-start(bf16[1,48,1536]{2,1,0:T(8,128)(2,1)S(1)} %get-tuple-element.49), channel_id=1, source_target_pairs={{0,1},{1,2},{2,3},{3,4},{4,5},{5,6},{6,7},{8,9},{9,10},{10,11},{11... | collective-permute-start | bytes 442376 | tf_op jit(solution)/shard_map/ppermute | solution.py:45
  7.9 4.7 %collective-permute-start.1 = (bf16[1,48,1536]{2,1,0:T(8,128)(2,1)S(1)}, bf16[1,48,1536]{2,1,0:T(8,128)(2,1)S(1)}, u32[]{:S(2)}, u32[]{:S(2)}) collective-permute-start(bf16[1,48,1536]{2,1,0:T(8,128)(2,1)S(1)} %get-tuple-element.50), channel_id=1, source_target_pairs={{1,0},{2,1},{3,2},{4,3},{5,4},{6,5},{7,6},{9,8},{10,9},{11,10},{12... | collective-permute-start | bytes 442376 | tf_op jit(solution)/shard_map/ppermute | solution.py:47
  12.7 1.7 collective-permute-done.1
  14.4 15.0 %collective-permute-start.2 = (bf16[1,224,1536]{2,1,0:T(8,128)(2,1)S(1)}, bf16[1,224,1536]{2,1,0:T(8,128)(2,1)S(1)}, u32[]{:S(2)}, u32[]{:S(2)}) collective-permute-start(bf16[1,224,1536]{2,1,0:T(8,128)(2,1)S(1)} %pad_maximum_fusion), channel_id=1, source_target_pairs={{0,384},{8,392},{16,400},{24,408},{32,416},{40,424},{48,432},{56,4... | collective-permute-start | bytes 2064392 | tf_op jit(solution)/shard_map/ppermute | solution.py:20
  29.8 1.3 collective-permute-start.3
  31.1 2.8 select_convert_fusion.mask_ref
  33.9 1.3 collective-permute-start.6
  35.2 1.3 collective-permute-start.5
  36.5 1.3 collective-permute-start.7
  37.8 14.1 %collective-permute-done.2 = bf16[1,224,1536]{2,1,0:T(8,128)(2,1)S(1)} collective-permute-done((bf16[1,224,1536]{2,1,0:T(8,128)(2,1)S(1)}, bf16[1,224,1536]{2,1,0:T(8,128)(2,1)S(1)}, u32[]{:S(2)}, u32[]{:S(2)}) %collective-permute-start.2) | collective-permute-done | bytes 688160 | tf_op jit(solution)/shard_map/ppermute | solution.py:20
  51.9 1.3 collective-permute-start.4
  53.3 11.9 %collective-permute-done.4 = bf16[1,224,1536]{2,1,0:T(8,128)(2,1)S(1)} collective-permute-done((bf16[1,224,1536]{2,1,0:T(8,128)(2,1)S(1)}, bf16[1,224,1536]{2,1,0:T(8,128)(2,1)S(1)}, u32[]{:S(2)}, u32[]{:S(2)}) %collective-permute-start.4) | collective-permute-done | bytes 688160 | tf_op jit(solution)/shard_map/ppermute | solution.py:20
  65.4 33.9 %collective-permute-done.6 = bf16[1,224,1536]{2,1,0:T(8,128)(2,1)S(1)} collective-permute-done((bf16[1,224,1536]{2,1,0:T(8,128)(2,1)S(1)}, bf16[1,224,1536]{2,1,0:T(8,128)(2,1)S(1)}, u32[]{:S(2)}, u32[]{:S(2)}) %collective-permute-start.6) | collective-permute-done | bytes 688160 | tf_op jit(solution)/shard_map/ppermute | solution.py:20
  99.4 2.3 copy-done
  101.7 34.9 %shard_map.83 = (bf16[128,768]{1,0:T(8,128)(2,1)}, bf16[128,768]{1,0:T(8,128)(2,1)}, f32[7,224,1536]{2,1,0:T(8,128)}, f32[1,128]{1,0:T(1,128)}) custom-call(bf16[128,768]{1,0:T(8,128)(2,1)} %bitcast.36, bf16[128,768]{1,0:T(8,128)(2,1)} %bitcast.37, bf16[7,224,1536]{2,1,0:T(8,128)(2,1)} %bitcast.35, f32[49,128,128]{2,1,0:T(8,128)} %select_convert_fusion.mask_ref), custom_call_target="tpu_custom_call" | custom-call | tf_op jit(solution)/shard_map/pallas_call | solution.py:164
  136.6 4.3 %convert.16 = bf16[7,224,1536]{2,1,0:T(8,128)(2,1)S(1)} convert(f32[7,224,1536]{2,1,0:T(8,128)} %get-tuple-element.35) | non-fusion elementwise | flops 2408448 | bytes 14450688 | tf_op jit(solution)/shard_map/convert.9
  141.2 1.3 collective-permute-start.8
  142.5 12.8 %collective-permute-start.13 = (bf16[1,224,1536]{2,1,0:T(8,128)(2,1)S(1)}, bf16[1,224,1536]{2,1,0:T(8,128)(2,1)S(1)}, u32[]{:S(2)}, u32[]{:S(2)}) collective-permute-start(bf16[1,224,1536]{2,1,0:T(8,128)(2,1)S(1)} %get-tuple-element.40), channel_id=1, source_target_pairs={{0,384},{8,392},{16,400},{24,408},{32,416},{40,424},{48,432},{56,4... | collective-permute-start | bytes 2064392 | tf_op jit(solution)/shard_map/ppermute | solution.py:20
  155.3 1.3 collective-permute-start.12
  156.6 2.2 collective-permute-start.11
  158.8 1.3 collective-permute-start.10
  160.1 19.2 %collective-permute-done.8 = bf16[1,224,1536]{2,1,0:T(8,128)(2,1)S(1)} collective-permute-done((bf16[1,224,1536]{2,1,0:T(8,128)(2,1)S(1)}, bf16[1,224,1536]{2,1,0:T(8,128)(2,1)S(1)}, u32[]{:S(2)}, u32[]{:S(2)}) %collective-permute-start.8) | collective-permute-done | bytes 688160 | tf_op jit(solution)/shard_map/ppermute | solution.py:20
  179.3 1.3 collective-permute-start.9
  180.6 1.9 collective-permute-start.16
  182.6 23.8 %collective-permute-done.12 = bf16[1,224,1536]{2,1,0:T(8,128)(2,1)S(1)} collective-permute-done((bf16[1,224,1536]{2,1,0:T(8,128)(2,1)S(1)}, bf16[1,224,1536]{2,1,0:T(8,128)(2,1)S(1)}, u32[]{:S(2)}, u32[]{:S(2)}) %collective-permute-start.12) | collective-permute-done | bytes 688160 | tf_op jit(solution)/shard_map/ppermute | solution.py:20
  206.4 8.0 %collective-permute-done.10 = bf16[1,224,1536]{2,1,0:T(8,128)(2,1)S(1)} collective-permute-done((bf16[1,224,1536]{2,1,0:T(8,128)(2,1)S(1)}, bf16[1,224,1536]{2,1,0:T(8,128)(2,1)S(1)}, u32[]{:S(2)}, u32[]{:S(2)}) %collective-permute-start.10) | collective-permute-done | bytes 688160 | tf_op jit(solution)/shard_map/ppermute | solution.py:20
  214.3 2.0 fusion.4
  216.3 1.9 collective-permute-start.14
  218.3 2.8 collective-permute-start.17
  221.1 1.5 collective-permute-done.17
  222.6 10.3 %collective-permute-start.18 = (f32[12]{0:T(128)S(1)}, f32[12]{0:T(128)S(1)}, u32[]{:S(2)}, u32[]{:S(2)}) collective-permute-start(f32[12]{0:T(128)S(1)} %max.28), channel_id=1, source_target_pairs={{0,4},{1,5},{2,6},{3,7},{4,0},{5,1},{6,2},{7,3},{8,12},{9,13},{10,... | collective-permute-start | bytes 152 | tf_op jit(solution)/shard_map/ppermute | solution.py:31
  232.9 0.9 collective-permute-done.18
  233.8 3.1 collective-permute-start.19
  236.9 1.2 collective-permute-done.19
  238.1 4.7 %collective-permute-start.20 = (f32[12]{0:T(128)S(1)}, f32[12]{0:T(128)S(1)}, u32[]{:S(2)}, u32[]{:S(2)}) collective-permute-start(f32[12]{0:T(128)S(1)} %max.30), channel_id=1, source_target_pairs={{0,16},{8,24},{16,0},{24,8},{32,48},{40,56},{48,32},{56,40},{64,80... | collective-permute-start | bytes 152 | tf_op jit(solution)/shard_map/ppermute | solution.py:31
  242.9 1.1 collective-permute-done.20
  243.9 28.7 %collective-permute-start.21 = (f32[12]{0:T(128)S(1)}, f32[12]{0:T(128)S(1)}, u32[]{:S(2)}, u32[]{:S(2)}) collective-permute-start(f32[12]{0:T(128)S(1)} %max.31), channel_id=1, source_target_pairs={{0,32},{8,40},{16,48},{24,56},{32,0},{40,8},{48,16},{56,24},{64,96... | collective-permute-start | bytes 152 | tf_op jit(solution)/shard_map/ppermute | solution.py:31
  272.7 0.9 collective-permute-done.21
  273.6 16.5 %collective-permute-start.22 = (f32[12]{0:T(128)S(1)}, f32[12]{0:T(128)S(1)}, u32[]{:S(2)}, u32[]{:S(2)}) collective-permute-start(f32[12]{0:T(128)S(1)} %max.32), channel_id=1, source_target_pairs={{0,64},{8,72},{16,80},{24,88},{32,96},{40,104},{48,112},{56,120},{... | collective-permute-start | bytes 152 | tf_op jit(solution)/shard_map/ppermute | solution.py:31
  290.1 0.9 collective-permute-done.22
  291.1 13.7 %collective-permute-start.23 = (f32[12]{0:T(128)S(1)}, f32[12]{0:T(128)S(1)}, u32[]{:S(2)}, u32[]{:S(2)}) collective-permute-start(f32[12]{0:T(128)S(1)} %max.33), channel_id=1, source_target_pairs={{0,128},{8,136},{16,144},{24,152},{32,160},{40,168},{48,176},{56,1... | collective-permute-start | bytes 152 | tf_op jit(solution)/shard_map/ppermute | solution.py:31
  304.8 0.9 collective-permute-done.23
  305.7 1.9 collective-permute-start.24
  307.6 6.3 %collective-permute-done.24 = f32[12]{0:T(128)S(1)} collective-permute-done((f32[12]{0:T(128)S(1)}, f32[12]{0:T(128)S(1)}, u32[]{:S(2)}, u32[]{:S(2)}) %collective-permute-start.24) | collective-permute-done | bytes 80 | tf_op jit(solution)/shard_map/ppermute | solution.py:31
  314.5 11.5 %collective-permute-start.15 = (bf16[1,48,1536]{2,1,0:T(8,128)(2,1)S(1)}, bf16[1,48,1536]{2,1,0:T(8,128)(2,1)S(1)}, u32[]{:S(2)}, u32[]{:S(2)}) collective-permute-start(bf16[1,48,1536]{2,1,0:T(8,128)(2,1)S(1)} %get-tuple-element.45), channel_id=1, source_target_pairs={{0,1},{1,2},{2,3},{3,4},{4,5},{5,6},{6,7},{8,9},{9,10},{10,11},{11... | collective-permute-start | bytes 442376 | tf_op jit(solution)/shard_map/ppermute | solution.py:20
  326.0 2.0 collective-permute-done.15
  (48 shorter events, 2.6 us)
Async XLA Ops:
  2.5 10.2 %collective-permute-start = (bf16[1,48,1536]{2,1,0:T(8,128)(2,1)S(1)}, bf16[1,48,1536]{2,1,0:T(8,128)(2,1)S(1)}, u32[]{:S(2)}, u32[]{:S(2)}) collective-permute-start(bf16[1,48,1536]{2,1,0:T(8,128)(2,1)S(1)} %get-tuple-element.49), channel_id=1, source_target_pairs={{0,1},{1,2},{2,3},{3,4},{4,5},{5,6},{6,7},{8,9},{9,10},{10,11},{11... | collective-permute-start | bytes 442376 | tf_op jit(solution)/shard_map/ppermute | solution.py:45
  7.9 6.5 %collective-permute-start.1 = (bf16[1,48,1536]{2,1,0:T(8,128)(2,1)S(1)}, bf16[1,48,1536]{2,1,0:T(8,128)(2,1)S(1)}, u32[]{:S(2)}, u32[]{:S(2)}) collective-permute-start(bf16[1,48,1536]{2,1,0:T(8,128)(2,1)S(1)} %get-tuple-element.50), channel_id=1, source_target_pairs={{1,0},{2,1},{3,2},{4,3},{5,4},{6,5},{7,6},{9,8},{10,9},{11,10},{12... | collective-permute-start | bytes 442376 | tf_op jit(solution)/shard_map/ppermute | solution.py:47
  14.4 37.4 %collective-permute-start.2 = (bf16[1,224,1536]{2,1,0:T(8,128)(2,1)S(1)}, bf16[1,224,1536]{2,1,0:T(8,128)(2,1)S(1)}, u32[]{:S(2)}, u32[]{:S(2)}) collective-permute-start(bf16[1,224,1536]{2,1,0:T(8,128)(2,1)S(1)} %pad_maximum_fusion), channel_id=1, source_target_pairs={{0,384},{8,392},{16,400},{24,408},{32,416},{40,424},{48,432},{56,4... | collective-permute-start | bytes 2064392 | tf_op jit(solution)/shard_map/ppermute | solution.py:20
  29.8 23.5 %collective-permute-start.3 = (bf16[1,224,1536]{2,1,0:T(8,128)(2,1)S(1)}, bf16[1,224,1536]{2,1,0:T(8,128)(2,1)S(1)}, u32[]{:S(2)}, u32[]{:S(2)}) collective-permute-start(bf16[1,224,1536]{2,1,0:T(8,128)(2,1)S(1)} %pad_maximum_fusion), channel_id=1, source_target_pairs={{0,256},{8,264},{16,272},{24,280},{32,288},{40,296},{48,304},{56,3... | collective-permute-start | bytes 2064392 | tf_op jit(solution)/shard_map/ppermute | solution.py:20
  33.9 65.4 %collective-permute-start.6 = (bf16[1,224,1536]{2,1,0:T(8,128)(2,1)S(1)}, bf16[1,224,1536]{2,1,0:T(8,128)(2,1)S(1)}, u32[]{:S(2)}, u32[]{:S(2)}) collective-permute-start(bf16[1,224,1536]{2,1,0:T(8,128)(2,1)S(1)} %pad_maximum_fusion), channel_id=1, source_target_pairs={{256,0},{264,8},{272,16},{280,24},{288,32},{296,40},{304,48},{312,... | collective-permute-start | bytes 2064392 | tf_op jit(solution)/shard_map/ppermute | solution.py:20
  35.2 30.2 %collective-permute-start.5 = (bf16[1,224,1536]{2,1,0:T(8,128)(2,1)S(1)}, bf16[1,224,1536]{2,1,0:T(8,128)(2,1)S(1)}, u32[]{:S(2)}, u32[]{:S(2)}) collective-permute-start(bf16[1,224,1536]{2,1,0:T(8,128)(2,1)S(1)} %pad_maximum_fusion), channel_id=1, source_target_pairs={{128,0},{136,8},{144,16},{152,24},{160,32},{168,40},{176,48},{184,... | collective-permute-start | bytes 2064392 | tf_op jit(solution)/shard_map/ppermute | solution.py:20
  36.5 62.9 %collective-permute-start.7 = (bf16[1,224,1536]{2,1,0:T(8,128)(2,1)S(1)}, bf16[1,224,1536]{2,1,0:T(8,128)(2,1)S(1)}, u32[]{:S(2)}, u32[]{:S(2)}) collective-permute-start(bf16[1,224,1536]{2,1,0:T(8,128)(2,1)S(1)} %pad_maximum_fusion), channel_id=1, source_target_pairs={{384,0},{392,8},{400,16},{408,24},{416,32},{424,40},{432,48},{440,... | collective-permute-start | bytes 2064392 | tf_op jit(solution)/shard_map/ppermute | solution.py:20
  51.9 13.4 %collective-permute-start.4 = (bf16[1,224,1536]{2,1,0:T(8,128)(2,1)S(1)}, bf16[1,224,1536]{2,1,0:T(8,128)(2,1)S(1)}, u32[]{:S(2)}, u32[]{:S(2)}) collective-permute-start(bf16[1,224,1536]{2,1,0:T(8,128)(2,1)S(1)} %pad_maximum_fusion), channel_id=1, source_target_pairs={{0,128},{8,136},{16,144},{24,152},{32,160},{40,168},{48,176},{56,1... | collective-permute-start | bytes 2064392 | tf_op jit(solution)/shard_map/ppermute | solution.py:20
  99.4 2.3 copy-start
  140.9 39.7 %copy-start.1 = (f32[1,128]{1,0:T(1,128)S(1)}, f32[1,128]{1,0:T(1,128)}, u32[]{:S(2)}) copy-start(f32[1,128]{1,0:T(1,128)} %get-tuple-element.36) | copy-start | bytes 1540
  141.2 38.1 %collective-permute-start.8 = (bf16[1,224,1536]{2,1,0:T(8,128)(2,1)S(1)}, bf16[1,224,1536]{2,1,0:T(8,128)(2,1)S(1)}, u32[]{:S(2)}, u32[]{:S(2)}) collective-permute-start(bf16[1,224,1536]{2,1,0:T(8,128)(2,1)S(1)} %get-tuple-element.39), channel_id=1, source_target_pairs={{384,0},{392,8},{400,16},{408,24},{416,32},{424,40},{432,48},{440,... | collective-permute-start | bytes 2064392 | tf_op jit(solution)/shard_map/ppermute | solution.py:20
  142.5 38.1 %collective-permute-start.13 = (bf16[1,224,1536]{2,1,0:T(8,128)(2,1)S(1)}, bf16[1,224,1536]{2,1,0:T(8,128)(2,1)S(1)}, u32[]{:S(2)}, u32[]{:S(2)}) collective-permute-start(bf16[1,224,1536]{2,1,0:T(8,128)(2,1)S(1)} %get-tuple-element.40), channel_id=1, source_target_pairs={{0,384},{8,392},{16,400},{24,408},{32,416},{40,424},{48,432},{56,4... | collective-permute-start | bytes 2064392 | tf_op jit(solution)/shard_map/ppermute | solution.py:20
  155.3 51.1 %collective-permute-start.12 = (bf16[1,224,1536]{2,1,0:T(8,128)(2,1)S(1)}, bf16[1,224,1536]{2,1,0:T(8,128)(2,1)S(1)}, u32[]{:S(2)}, u32[]{:S(2)}) collective-permute-start(bf16[1,224,1536]{2,1,0:T(8,128)(2,1)S(1)} %get-tuple-element.41), channel_id=1, source_target_pairs={{0,256},{8,264},{16,272},{24,280},{32,288},{40,296},{48,304},{56,3... | collective-permute-start | bytes 2064392 | tf_op jit(solution)/shard_map/ppermute | solution.py:20
  156.6 49.7 %collective-permute-start.11 = (bf16[1,224,1536]{2,1,0:T(8,128)(2,1)S(1)}, bf16[1,224,1536]{2,1,0:T(8,128)(2,1)S(1)}, u32[]{:S(2)}, u32[]{:S(2)}) collective-permute-start(bf16[1,224,1536]{2,1,0:T(8,128)(2,1)S(1)} %get-tuple-element.42), channel_id=1, source_target_pairs={{0,128},{8,136},{16,144},{24,152},{32,160},{40,168},{48,176},{56,1... | collective-permute-start | bytes 2064392 | tf_op jit(solution)/shard_map/ppermute | solution.py:20
  158.8 55.5 %collective-permute-start.10 = (bf16[1,224,1536]{2,1,0:T(8,128)(2,1)S(1)}, bf16[1,224,1536]{2,1,0:T(8,128)(2,1)S(1)}, u32[]{:S(2)}, u32[]{:S(2)}) collective-permute-start(bf16[1,224,1536]{2,1,0:T(8,128)(2,1)S(1)} %get-tuple-element.43), channel_id=1, source_target_pairs={{128,0},{136,8},{144,16},{152,24},{160,32},{168,40},{176,48},{184,... | collective-permute-start | bytes 2064392 | tf_op jit(solution)/shard_map/ppermute | solution.py:20
  179.3 35.0 %collective-permute-start.9 = (bf16[1,224,1536]{2,1,0:T(8,128)(2,1)S(1)}, bf16[1,224,1536]{2,1,0:T(8,128)(2,1)S(1)}, u32[]{:S(2)}, u32[]{:S(2)}) collective-permute-start(bf16[1,224,1536]{2,1,0:T(8,128)(2,1)S(1)} %get-tuple-element.44), channel_id=1, source_target_pairs={{256,0},{264,8},{272,16},{280,24},{288,32},{296,40},{304,48},{312,... | collective-permute-start | bytes 2064392 | tf_op jit(solution)/shard_map/ppermute | solution.py:20
  180.6 37.6 %collective-permute-start.16 = (f32[12]{0:T(128)S(1)}, f32[12]{0:T(128)S(1)}, u32[]{:S(2)}, u32[]{:S(2)}) collective-permute-start(f32[12]{0:T(128)S(1)} %slice_bitcast_fusion), channel_id=1, source_target_pairs={{0,1},{1,0},{2,3},{3,2},{4,5},{5,4},{6,7},{7,6},{8,9},{9,8},{10,11... | collective-permute-start | bytes 152 | tf_op jit(solution)/shard_map/ppermute | solution.py:31
  216.3 109.7 %collective-permute-start.14 = (bf16[1,48,1536]{2,1,0:T(8,128)(2,1)S(1)}, bf16[1,48,1536]{2,1,0:T(8,128)(2,1)S(1)}, u32[]{:S(2)}, u32[]{:S(2)}) collective-permute-start(bf16[1,48,1536]{2,1,0:T(8,128)(2,1)S(1)} %get-tuple-element.46), channel_id=1, source_target_pairs={{1,0},{2,1},{3,2},{4,3},{5,4},{6,5},{7,6},{9,8},{10,9},{11,10},{12... | collective-permute-start | bytes 442376 | tf_op jit(solution)/shard_map/ppermute | solution.py:20
  218.3 4.3 %collective-permute-start.17 = (f32[12]{0:T(128)S(1)}, f32[12]{0:T(128)S(1)}, u32[]{:S(2)}, u32[]{:S(2)}) collective-permute-start(f32[12]{0:T(128)S(1)} %fusion.3), channel_id=1, source_target_pairs={{0,2},{1,3},{2,0},{3,1},{4,6},{5,7},{6,4},{7,5},{8,10},{9,11},{10,... | collective-permute-start | bytes 152 | tf_op jit(solution)/shard_map/ppermute | solution.py:31
  222.6 11.2 %collective-permute-start.18 = (f32[12]{0:T(128)S(1)}, f32[12]{0:T(128)S(1)}, u32[]{:S(2)}, u32[]{:S(2)}) collective-permute-start(f32[12]{0:T(128)S(1)} %max.28), channel_id=1, source_target_pairs={{0,4},{1,5},{2,6},{3,7},{4,0},{5,1},{6,2},{7,3},{8,12},{9,13},{10,... | collective-permute-start | bytes 152 | tf_op jit(solution)/shard_map/ppermute | solution.py:31
  233.8 4.3 %collective-permute-start.19 = (f32[12]{0:T(128)S(1)}, f32[12]{0:T(128)S(1)}, u32[]{:S(2)}, u32[]{:S(2)}) collective-permute-start(f32[12]{0:T(128)S(1)} %max.29), channel_id=1, source_target_pairs={{0,8},{8,0},{16,24},{24,16},{32,40},{40,32},{48,56},{56,48},{64,72... | collective-permute-start | bytes 152 | tf_op jit(solution)/shard_map/ppermute | solution.py:31
  238.1 5.8 %collective-permute-start.20 = (f32[12]{0:T(128)S(1)}, f32[12]{0:T(128)S(1)}, u32[]{:S(2)}, u32[]{:S(2)}) collective-permute-start(f32[12]{0:T(128)S(1)} %max.30), channel_id=1, source_target_pairs={{0,16},{8,24},{16,0},{24,8},{32,48},{40,56},{48,32},{56,40},{64,80... | collective-permute-start | bytes 152 | tf_op jit(solution)/shard_map/ppermute | solution.py:31
  243.9 29.7 %collective-permute-start.21 = (f32[12]{0:T(128)S(1)}, f32[12]{0:T(128)S(1)}, u32[]{:S(2)}, u32[]{:S(2)}) collective-permute-start(f32[12]{0:T(128)S(1)} %max.31), channel_id=1, source_target_pairs={{0,32},{8,40},{16,48},{24,56},{32,0},{40,8},{48,16},{56,24},{64,96... | collective-permute-start | bytes 152 | tf_op jit(solution)/shard_map/ppermute | solution.py:31
  273.6 17.4 %collective-permute-start.22 = (f32[12]{0:T(128)S(1)}, f32[12]{0:T(128)S(1)}, u32[]{:S(2)}, u32[]{:S(2)}) collective-permute-start(f32[12]{0:T(128)S(1)} %max.32), channel_id=1, source_target_pairs={{0,64},{8,72},{16,80},{24,88},{32,96},{40,104},{48,112},{56,120},{... | collective-permute-start | bytes 152 | tf_op jit(solution)/shard_map/ppermute | solution.py:31
  291.1 14.7 %collective-permute-start.23 = (f32[12]{0:T(128)S(1)}, f32[12]{0:T(128)S(1)}, u32[]{:S(2)}, u32[]{:S(2)}) collective-permute-start(f32[12]{0:T(128)S(1)} %max.33), channel_id=1, source_target_pairs={{0,128},{8,136},{16,144},{24,152},{32,160},{40,168},{48,176},{56,1... | collective-permute-start | bytes 152 | tf_op jit(solution)/shard_map/ppermute | solution.py:31
  305.7 8.2 %collective-permute-start.24 = (f32[12]{0:T(128)S(1)}, f32[12]{0:T(128)S(1)}, u32[]{:S(2)}, u32[]{:S(2)}) collective-permute-start(f32[12]{0:T(128)S(1)} %max.34), channel_id=1, source_target_pairs={{0,256},{8,264},{16,272},{24,280},{32,288},{40,296},{48,304},{56,3... | collective-permute-start | bytes 152 | tf_op jit(solution)/shard_map/ppermute | solution.py:31
  314.5 13.5 %collective-permute-start.15 = (bf16[1,48,1536]{2,1,0:T(8,128)(2,1)S(1)}, bf16[1,48,1536]{2,1,0:T(8,128)(2,1)S(1)}, u32[]{:S(2)}, u32[]{:S(2)}) collective-permute-start(bf16[1,48,1536]{2,1,0:T(8,128)(2,1)S(1)} %get-tuple-element.45), channel_id=1, source_target_pairs={{0,1},{1,2},{2,3},{3,4},{4,5},{5,6},{6,7},{8,9},{9,10},{10,11},{11... | collective-permute-start | bytes 442376 | tf_op jit(solution)/shard_map/ppermute | solution.py:20
where the time goes:
time: 331 us; the launch traced here: 329 us
  starting transfers between devices  149 us (45%)
  waiting for transfers between devices  128 us (39%)
  Pallas kernels  34.9 us (11%)
  other arithmetic  10 us (3%)
  local copies, waits for them, and re-layouts  5.75 us (2%)
    ppermute x14, waiting for transfers between devices, passed_along(): lax.ppermute(value, axis, [(source, source + steps) for source in range(f...  113 us
    ppermute x9, starting transfers between devices, all_max(): partner = lax.ppermute(value, axis, [(i, i ^ stride) for i in range(count)])  83.7 us
    ppermute x14, starting transfers between devices, passed_along(): lax.ppermute(value, axis, [(source, source + steps) for source in range(f...  55.1 us
    pallas_call x1, Pallas kernels, neighbourhood_kernel(): pl.pallas_call(neighbourhood_body, out_shape=(jax.ShapeDtypeStruct((token...  34.9 us
    ppermute x9, waiting for transfers between devices, all_max(): partner = lax.ppermute(value, axis, [(i, i ^ stride) for i in range(count)])  13.8 us
  transfers between devices with their start and end apart: 25, of which 16 were waited for; matrix products, arithmetic and copies ran while one was open for 2% of the time, Pallas kernels for 0%

commit v1 on v0

--- a/solution.py
+++ b/solution.py
@@ -28,9 +28,18 @@
             continue
         stride = 1
         while stride < count:
-            partner = lax.ppermute(value, axis, [(i, i ^ stride) for i in range(count)])
-            value = jnp.maximum(value, partner)
-            stride *= 2
+            radix = min(8, count // stride)
+            group = stride * radix
+            parts = [value]
+            for step in range(1, radix):
+                pairs = [
+                    (i, (i // group) * group + ((i // stride + step) % radix) * stride + i % stride)
+                    for i in range(count)
+                ]
+                parts.append(lax.ppermute(value, axis, pairs))
+            for part in parts[1:]:
+                value = jnp.maximum(value, part)
+            stride = group
     return value
 
 
@@ -195,8 +204,7 @@
     col_usable = (col_target >= 0) & (col_target < col_total)
     usable = col_usable[:, None, None, :] & row_usable[None, :, :, None]
     pairs_in = jnp.concatenate([key_vectors, value_vectors], axis=-1)
-    widened = extended(pairs_in, (("col", 1),), neighbour_cells)
-    stacked = spread_pairs(widened, step_length)
+    stacked = extended(spread_pairs(pairs_in, step_length), (("col", 2),), neighbour_cells)
 
     tokens = lax.broadcasted_iota(jnp.int32, (window * window, token_count, LANES), 2) < H
     usable_ab = jnp.transpose(usable[:, :, 0, :], (1, 0, 2)).reshape(window * window, token_count)
@@ -211,14 +219,14 @@
     query_grad = query_grad.reshape(rows_per_shard, cols_dev, feature_count)
     logit_peak = all_max(peak[0, :H], ("col", "row"))
     spill = spill.reshape(window, rows_per_shard, cols_dev + 2 * neighbour_cells, 2 * feature_count)
-    gathered = return_rows(spill, step_length)
-    west_part = gathered[:, :neighbour_cells]
-    east_part = gathered[:, neighbour_cells + cols_dev :]
-    owned = gathered[:, neighbour_cells : neighbour_cells + cols_dev]
+    west_part = spill[:, :, :neighbour_cells]
+    east_part = spill[:, :, neighbour_cells + cols_dev :]
+    owned = spill[:, :, neighbour_cells : neighbour_cells + cols_dev]
     from_east = passed_along(west_part.astype(jnp.bfloat16), "col", -1).astype(west_part.dtype)
     from_west = passed_along(east_part.astype(jnp.bfloat16), "col", 1).astype(east_part.dtype)
-    owned = owned.at[:, cols_dev - neighbour_cells :].add(from_east)
-    owned = owned.at[:, :neighbour_cells].add(from_west)
+    owned = owned.at[:, :, cols_dev - neighbour_cells :].add(from_east)
+    owned = owned.at[:, :, :neighbour_cells].add(from_west)
+    owned = return_rows(owned, step_length)
     key_grad = owned[..., :feature_count].astype(jnp.bfloat16)
     value_grad = owned[..., feature_count:].astype(jnp.bfloat16)
     return (attended, query_grad, key_grad, value_grad, logit_peak)

time: 331 us -> 308 us (0.931)
  the two profiles are of different devices: /device:TPU:1 before, /device:TPU:104 now
where the time goes in v1:
time: 308 us; the launch traced here: 307 us
  starting transfers between devices  178 us (58%)
  waiting for transfers between devices  69.1 us (22%)
  Pallas kernels  34.9 us (11%)
  other arithmetic  14 us (5%)
  local copies, waits for them, and re-layouts  9.24 us (3%)
    ppermute x21, starting transfers between devices, all_max(): parts.append(lax.ppermute(value, axis, pairs))  91.7 us
    ppermute x14, starting transfers between devices, passed_along(): lax.ppermute(value, axis, [(source, source + steps) for source in range(f...  81 us
    ppermute x14, waiting for transfers between devices, passed_along(): lax.ppermute(value, axis, [(source, source + steps) for source in range(f...  53.3 us
    pallas_call x1, Pallas kernels, neighbourhood_kernel(): pl.pallas_call(neighbourhood_body, out_shape=(jax.ShapeDtypeStruct((token...  34.9 us
    ppermute x1, waiting for transfers between devices, extended(): lax.ppermute(tail, axis, [(i, (i + 1) % count) for i in range(ends)])  7.57 us
    ppermute x21, waiting for transfers between devices, all_max(): parts.append(lax.ppermute(value, axis, pairs))  6.55 us
  transfers between devices with their start and end apart: 37, of which 10 were waited for; matrix products, arithmetic and copies ran while one was open for 3% of the time, Pallas kernels for 0%

profile of v1, /device:TPU:104, one launch (start us, length us, event | category | flops | bytes accessed | tf_op | source)
XLA Modules:
  0.0 306.8 jit_solution(10873853028087299869)
XLA Ops:
  2.5 1.4 collective-permute-start
  4.6 1.3 collective-permute-start.4
  5.9 17.2 %collective-permute-start.3 = (bf16[1,128,1536]{2,1,0:T(8,128)(2,1)S(1)}, bf16[1,128,1536]{2,1,0:T(8,128)(2,1)}, u32[]{:S(2)}, u32[]{:S(2)}) collective-permute-start(bf16[1,128,1536]{2,1,0:T(8,128)(2,1)S(1)} %constant_dynamic-update-slice_fusion), channel_id=1, source_target_pairs={{128,0},{136,8},{144,16},{152,24},{160,32},{168,40},{176,48},{184,... | collective-permute-start | bytes 1179656 | tf_op jit(solution)/shard_map/ppermute | solution.py:20
  23.2 8.6 %collective-permute-start.2 = (bf16[1,128,1536]{2,1,0:T(8,128)(2,1)S(1)}, bf16[1,128,1536]{2,1,0:T(8,128)(2,1)}, u32[]{:S(2)}, u32[]{:S(2)}) collective-permute-start(bf16[1,128,1536]{2,1,0:T(8,128)(2,1)S(1)} %constant_dynamic-update-slice_fusion), channel_id=1, source_target_pairs={{0,128},{8,136},{16,144},{24,152},{32,160},{40,168},{48,176},{56,1... | collective-permute-start | bytes 1179656 | tf_op jit(solution)/shard_map/ppermute | solution.py:20
  31.9 27.2 %collective-permute-start.1 = (bf16[1,128,1536]{2,1,0:T(8,128)(2,1)S(1)}, bf16[1,128,1536]{2,1,0:T(8,128)(2,1)S(1)}, u32[]{:S(2)}, u32[]{:S(2)}) collective-permute-start(bf16[1,128,1536]{2,1,0:T(8,128)(2,1)S(1)} %constant_dynamic-update-slice_fusion), channel_id=1, source_target_pairs={{0,256},{8,264},{16,272},{24,280},{32,288},{40,296},{48,304},{56,3... | collective-permute-start | bytes 1179656 | tf_op jit(solution)/shard_map/ppermute | solution.py:20
  60.0 15.1 %collective-permute-done.1 = bf16[1,128,1536]{2,1,0:T(8,128)(2,1)S(1)} collective-permute-done((bf16[1,128,1536]{2,1,0:T(8,128)(2,1)S(1)}, bf16[1,128,1536]{2,1,0:T(8,128)(2,1)S(1)}, u32[]{:S(2)}, u32[]{:S(2)}) %collective-permute-start.1) | collective-permute-done | bytes 393248 | tf_op jit(solution)/shard_map/ppermute | solution.py:20
  75.1 1.0 bitcast_dynamic-update-slice_fusion.3
  76.2 1.0 bitcast_dynamic-update-slice_fusion.1
  78.3 1.5 fusion.11
  79.8 1.9 collective-permute-start.6
  81.7 3.6 %collective-permute-start.7 = (bf16[7,1,48,1536]{3,2,0,1:T(8,128)(2,1)}, bf16[7,1,48,1536]{3,2,0,1:T(8,128)(2,1)}, u32[]{:S(2)}, u32[]{:S(2)}) collective-permute-start(bf16[7,1,48,1536]{3,2,0,1:T(8,128)(2,1)} %get-tuple-element.45), channel_id=1, source_target_pairs={{1,0},{2,1},{3,2},{4,3},{5,4},{6,5},{7,6},{9,8},{10,9},{11,10},{12... | collective-permute-start | bytes 3096584 | tf_op jit(solution)/shard_map/ppermute | solution.py:56
  85.7 2.7 select_convert_fusion.mask_ref
  88.5 7.6 %collective-permute-done.6 = bf16[7,1,48,1536]{3,2,0,1:T(8,128)(2,1)} collective-permute-done((bf16[7,1,48,1536]{3,2,0,1:T(8,128)(2,1)}, bf16[7,1,48,1536]{3,2,0,1:T(8,128)(2,1)}, u32[]{:S(2)}, u32[]{:S(2)}) %collective-permute-start.6) | collective-permute-done | bytes 1032224 | tf_op jit(solution)/shard_map/ppermute | solution.py:54
  96.0 1.8 collective-permute-done.7
  97.8 4.2 %maximum_bitcast_fusion.kv_ref = bf16[7,224,1536]{2,1,0:T(8,128)(2,1)} fusion(bf16[7,1,48,1536]{3,2,0,1:T(8,128)(2,1)} %collective-permute-done.7, bf16[7,1,128,1536]{3,2,0,1:T(8,128)(2,1)S(1)} %bitcast_dynamic-update-slice_fusion.6, bf16[7,1,48,1536]{3,2,0,1:T(8,128)(2,1)} %collective-permute-done.6), kind=kLoop, calls=%fused_computation | loop fusion | flops 14450688 | bytes 9633792 | tf_op jit(solution)/shard_map/reshape | solution.py:215
  102.0 34.9 %shard_map.83 = (bf16[128,768]{1,0:T(8,128)(2,1)}, bf16[128,768]{1,0:T(8,128)(2,1)}, f32[7,224,1536]{2,1,0:T(8,128)}, f32[1,128]{1,0:T(1,128)}) custom-call(bf16[128,768]{1,0:T(8,128)(2,1)} %bitcast.74, bf16[128,768]{1,0:T(8,128)(2,1)} %bitcast.75, bf16[7,224,1536]{2,1,0:T(8,128)(2,1)} %maximum_bitcast_fusion.kv_ref, f32[49,128,128]{2,1,0:T(8,128)} %select_convert_fusion.mask_ref), custom_call_target="tpu_custom_call" | custom-call | tf_op jit(solution)/shard_map/pallas_call | solution.py:173
  136.9 4.5 %bitcast_convert_fusion = bf16[7,1,224,1536]{3,2,0,1:T(8,128)(2,1)S(1)} fusion(f32[7,224,1536]{2,1,0:T(8,128)} %get-tuple-element.35), kind=kLoop, calls=%fused_computation.41 | loop fusion | flops 2408448 | bytes 14450688 | tf_op jit(solution)/shard_map/convert.9
  141.6 4.1 %collective-permute-start.8 = (bf16[7,1,48,1536]{3,2,0,1:T(8,128)(2,1)S(1)}, bf16[7,1,48,1536]{3,2,0,1:T(8,128)(2,1)S(1)}, u32[]{:S(2)}, u32[]{:S(2)}) collective-permute-start(bf16[7,1,48,1536]{3,2,0,1:T(8,128)(2,1)S(1)} %get-tuple-element.38), channel_id=1, source_target_pairs={{1,0},{2,1},{3,2},{4,3},{5,4},{6,5},{7,6},{9,8},{10,9},{11,10},{12... | collective-permute-start | bytes 3096584 | tf_op jit(solution)/shard_map/ppermute | solution.py:20
  145.7 1.9 collective-permute-start.21
  147.7 8.8 %collective-permute-start.20 = (f32[12]{0:T(128)S(1)}, f32[12]{0:T(128)S(1)}, u32[]{:S(2)}, u32[]{:S(2)}) collective-permute-start(f32[12]{0:T(128)S(1)} %slice_bitcast_fusion.7), channel_id=1, source_target_pairs={{0,5},{1,6},{2,7},{3,0},{4,1},{5,2},{6,3},{7,4},{8,13},{9,14},{10,... | collective-permute-start | bytes 152 | tf_op jit(solution)/shard_map/ppermute | solution.py:39
  156.5 4.0 %collective-permute-start.19 = (f32[12]{0:T(128)S(1)}, f32[12]{0:T(128)S(1)}, u32[]{:S(2)}, u32[]{:S(2)}) collective-permute-start(f32[12]{0:T(128)S(1)} %slice_bitcast_fusion.7), channel_id=1, source_target_pairs={{0,4},{1,5},{2,6},{3,7},{4,0},{5,1},{6,2},{7,3},{8,12},{9,13},{10,... | collective-permute-start | bytes 152 | tf_op jit(solution)/shard_map/ppermute | solution.py:39
  160.5 4.3 %collective-permute-start.18 = (f32[12]{0:T(128)S(1)}, f32[12]{0:T(128)S(1)}, u32[]{:S(2)}, u32[]{:S(2)}) collective-permute-start(f32[12]{0:T(128)S(1)} %slice_bitcast_fusion.7), channel_id=1, source_target_pairs={{0,3},{1,4},{2,5},{3,6},{4,7},{5,0},{6,1},{7,2},{8,11},{9,12},{10,... | collective-permute-start | bytes 152 | tf_op jit(solution)/shard_map/ppermute | solution.py:39
  165.8 1.9 collective-permute-start.17
  167.8 1.9 collective-permute-start.22
  169.7 2.4 collective-permute-start.16
  172.1 2.6 collective-permute-start.9
  175.0 1.9 collective-permute-start.29
  176.9 1.9 collective-permute-start.28
  178.8 7.2 %collective-permute-start.27 = (f32[12]{0:T(128)S(1)}, f32[12]{0:T(128)S(1)}, u32[]{:S(2)}, u32[]{:S(2)}) collective-permute-start(f32[12]{0:T(128)S(1)} %maximum_maximum_fusion.2), channel_id=1, source_target_pairs={{0,40},{8,48},{16,56},{24,0},{32,8},{40,16},{48,24},{56,32},{64,10... | collective-permute-start | bytes 152 | tf_op jit(solution)/shard_map/ppermute | solution.py:39
  186.1 1.9 collective-permute-start.26
  188.0 4.8 %collective-permute-start.25 = (f32[12]{0:T(128)S(1)}, f32[12]{0:T(128)S(1)}, u32[]{:S(2)}, u32[]{:S(2)}) collective-permute-start(f32[12]{0:T(128)S(1)} %maximum_maximum_fusion.2), channel_id=1, source_target_pairs={{0,24},{8,32},{16,40},{24,48},{32,56},{40,0},{48,8},{56,16},{64,88... | collective-permute-start | bytes 152 | tf_op jit(solution)/shard_map/ppermute | solution.py:39
  192.9 4.3 %collective-permute-start.24 = (f32[12]{0:T(128)S(1)}, f32[12]{0:T(128)S(1)}, u32[]{:S(2)}, u32[]{:S(2)}) collective-permute-start(f32[12]{0:T(128)S(1)} %maximum_maximum_fusion.2), channel_id=1, source_target_pairs={{0,16},{8,24},{16,32},{24,40},{32,48},{40,56},{48,0},{56,8},{64,80... | collective-permute-start | bytes 152 | tf_op jit(solution)/shard_map/ppermute | solution.py:39
  197.2 1.9 collective-permute-start.23
  199.1 1.6 collective-permute-done.24
  200.7 4.0 %collective-permute-done.23 = f32[12]{0:T(128)S(1)} collective-permute-done((f32[12]{0:T(128)S(1)}, f32[12]{0:T(128)S(1)}, u32[]{:S(2)}, u32[]{:S(2)}) %collective-permute-start.23) | collective-permute-done | bytes 80 | tf_op jit(solution)/shard_map/ppermute | solution.py:39
  204.8 1.9 collective-permute-start.36
  206.7 7.1 %collective-permute-start.35 = (f32[12]{0:T(128)S(1)}, f32[12]{0:T(128)S(1)}, u32[]{:S(2)}, u32[]{:S(2)}) collective-permute-start(f32[12]{0:T(128)S(1)} %maximum_maximum_fusion.1), channel_id=1, source_target_pairs={{0,384},{8,392},{16,400},{24,408},{32,416},{40,424},{48,432},{56,4... | collective-permute-start | bytes 152 | tf_op jit(solution)/shard_map/ppermute | solution.py:39
  213.8 10.6 %collective-permute-start.34 = (f32[12]{0:T(128)S(1)}, f32[12]{0:T(128)S(1)}, u32[]{:S(2)}, u32[]{:S(2)}) collective-permute-start(f32[12]{0:T(128)S(1)} %maximum_maximum_fusion.1), channel_id=1, source_target_pairs={{0,320},{8,328},{16,336},{24,344},{32,352},{40,360},{48,368},{56,3... | collective-permute-start | bytes 152 | tf_op jit(solution)/shard_map/ppermute | solution.py:39
  224.4 1.9 collective-permute-start.33
  228.8 8.5 %collective-permute-start.32 = (f32[12]{0:T(128)S(1)}, f32[12]{0:T(128)S(1)}, u32[]{:S(2)}, u32[]{:S(2)}) collective-permute-start(f32[12]{0:T(128)S(1)} %maximum_maximum_fusion.1), channel_id=1, source_target_pairs={{0,192},{8,200},{16,208},{24,216},{32,224},{40,232},{48,240},{56,2... | collective-permute-start | bytes 152 | tf_op jit(solution)/shard_map/ppermute | solution.py:39
  237.3 8.5 %collective-permute-start.31 = (f32[12]{0:T(128)S(1)}, f32[12]{0:T(128)S(1)}, u32[]{:S(2)}, u32[]{:S(2)}) collective-permute-start(f32[12]{0:T(128)S(1)} %maximum_maximum_fusion.1), channel_id=1, source_target_pairs={{0,128},{8,136},{16,144},{24,152},{32,160},{40,168},{48,176},{56,1... | collective-permute-start | bytes 152 | tf_op jit(solution)/shard_map/ppermute | solution.py:39
  245.9 3.8 %collective-permute-start.30 = (f32[12]{0:T(128)S(1)}, f32[12]{0:T(128)S(1)}, u32[]{:S(2)}, u32[]{:S(2)}) collective-permute-start(f32[12]{0:T(128)S(1)} %maximum_maximum_fusion.1), channel_id=1, source_target_pairs={{0,64},{8,72},{16,80},{24,88},{32,96},{40,104},{48,112},{56,120},{... | collective-permute-start | bytes 152 | tf_op jit(solution)/shard_map/ppermute | solution.py:39
  249.7 1.3 collective-permute-start.14
  251.0 4.9 %collective-permute-start.13 = (bf16[1,128,1536]{2,1,0:T(8,128)(2,1)S(1)}, bf16[1,128,1536]{2,1,0:T(8,128)(2,1)S(1)}, u32[]{:S(2)}, u32[]{:S(2)}) collective-permute-start(bf16[1,128,1536]{2,1,0:T(8,128)(2,1)S(1)} %get-tuple-element.41), channel_id=1, source_target_pairs={{0,128},{8,136},{16,144},{24,152},{32,160},{40,168},{48,176},{56,1... | collective-permute-start | bytes 1179656 | tf_op jit(solution)/shard_map/ppermute | solution.py:20
  256.0 9.0 %collective-permute-start.12 = (bf16[1,128,1536]{2,1,0:T(8,128)(2,1)S(1)}, bf16[1,128,1536]{2,1,0:T(8,128)(2,1)S(1)}, u32[]{:S(2)}, u32[]{:S(2)}) collective-permute-start(bf16[1,128,1536]{2,1,0:T(8,128)(2,1)S(1)} %get-tuple-element.42), channel_id=1, source_target_pairs={{128,0},{136,8},{144,16},{152,24},{160,32},{168,40},{176,48},{184,... | collective-permute-start | bytes 1179656 | tf_op jit(solution)/shard_map/ppermute | solution.py:20
  265.0 1.3 collective-permute-start.11
  268.1 31.7 %collective-permute-done.12 = bf16[1,128,1536]{2,1,0:T(8,128)(2,1)S(1)} collective-permute-done((bf16[1,128,1536]{2,1,0:T(8,128)(2,1)S(1)}, bf16[1,128,1536]{2,1,0:T(8,128)(2,1)S(1)}, u32[]{:S(2)}, u32[]{:S(2)}) %collective-permute-start.12) | collective-permute-done | bytes 393248 | tf_op jit(solution)/shard_map/ppermute | solution.py:20
  299.8 5.9 %collective-permute-done.11 = bf16[1,128,1536]{2,1,0:T(8,128)(2,1)S(1)} collective-permute-done((bf16[1,128,1536]{2,1,0:T(8,128)(2,1)S(1)}, bf16[1,128,1536]{2,1,0:T(8,128)(2,1)S(1)}, u32[]{:S(2)}, u32[]{:S(2)}) %collective-permute-start.11) | collective-permute-done | bytes 393248 | tf_op jit(solution)/shard_map/ppermute | solution.py:20
  (73 shorter events, 11.7 us)
Async XLA Ops:
  2.5 29.3 %collective-permute-start = (bf16[1,128,1536]{2,1,0:T(8,128)(2,1)S(1)}, bf16[1,128,1536]{2,1,0:T(8,128)(2,1)}, u32[]{:S(2)}, u32[]{:S(2)}) collective-permute-start(bf16[1,128,1536]{2,1,0:T(8,128)(2,1)S(1)} %constant_dynamic-update-slice_fusion), channel_id=1, source_target_pairs={{0,384},{8,392},{16,400},{24,408},{32,416},{40,424},{48,432},{56,4... | collective-permute-start | bytes 1179656 | tf_op jit(solution)/shard_map/ppermute | solution.py:20
  4.0 74.3 %collective-permute-start.5 = (bf16[1,128,1536]{2,1,0:T(8,128)(2,1)S(1)}, bf16[1,128,1536]{2,1,0:T(8,128)(2,1)S(1)}, u32[]{:S(2)}, u32[]{:S(2)}) collective-permute-start(bf16[1,128,1536]{2,1,0:T(8,128)(2,1)S(1)} %constant_dynamic-update-slice_fusion), channel_id=1, source_target_pairs={{384,0},{392,8},{400,16},{408,24},{416,32},{424,40},{432,48},{440,... | collective-permute-start | bytes 1179656 | tf_op jit(solution)/shard_map/ppermute | solution.py:20
  4.6 72.6 %collective-permute-start.4 = (bf16[1,128,1536]{2,1,0:T(8,128)(2,1)S(1)}, bf16[1,128,1536]{2,1,0:T(8,128)(2,1)}, u32[]{:S(2)}, u32[]{:S(2)}) collective-permute-start(bf16[1,128,1536]{2,1,0:T(8,128)(2,1)S(1)} %constant_dynamic-update-slice_fusion), channel_id=1, source_target_pairs={{256,0},{264,8},{272,16},{280,24},{288,32},{296,40},{304,48},{312,... | collective-permute-start | bytes 1179656 | tf_op jit(solution)/shard_map/ppermute | solution.py:20
  5.9 70.3 %collective-permute-start.3 = (bf16[1,128,1536]{2,1,0:T(8,128)(2,1)S(1)}, bf16[1,128,1536]{2,1,0:T(8,128)(2,1)}, u32[]{:S(2)}, u32[]{:S(2)}) collective-permute-start(bf16[1,128,1536]{2,1,0:T(8,128)(2,1)S(1)} %constant_dynamic-update-slice_fusion), channel_id=1, source_target_pairs={{128,0},{136,8},{144,16},{152,24},{160,32},{168,40},{176,48},{184,... | collective-permute-start | bytes 1179656 | tf_op jit(solution)/shard_map/ppermute | solution.py:20
  23.2 51.9 %collective-permute-start.2 = (bf16[1,128,1536]{2,1,0:T(8,128)(2,1)S(1)}, bf16[1,128,1536]{2,1,0:T(8,128)(2,1)}, u32[]{:S(2)}, u32[]{:S(2)}) collective-permute-start(bf16[1,128,1536]{2,1,0:T(8,128)(2,1)S(1)} %constant_dynamic-update-slice_fusion), channel_id=1, source_target_pairs={{0,128},{8,136},{16,144},{24,152},{32,160},{40,168},{48,176},{56,1... | collective-permute-start | bytes 1179656 | tf_op jit(solution)/shard_map/ppermute | solution.py:20
  31.9 43.2 %collective-permute-start.1 = (bf16[1,128,1536]{2,1,0:T(8,128)(2,1)S(1)}, bf16[1,128,1536]{2,1,0:T(8,128)(2,1)S(1)}, u32[]{:S(2)}, u32[]{:S(2)}) collective-permute-start(bf16[1,128,1536]{2,1,0:T(8,128)(2,1)S(1)} %constant_dynamic-update-slice_fusion), channel_id=1, source_target_pairs={{0,256},{8,264},{16,272},{24,280},{32,288},{40,296},{48,304},{56,3... | collective-permute-start | bytes 1179656 | tf_op jit(solution)/shard_map/ppermute | solution.py:20
  79.8 16.2 %collective-permute-start.6 = (bf16[7,1,48,1536]{3,2,0,1:T(8,128)(2,1)}, bf16[7,1,48,1536]{3,2,0,1:T(8,128)(2,1)}, u32[]{:S(2)}, u32[]{:S(2)}) collective-permute-start(bf16[7,1,48,1536]{3,2,0,1:T(8,128)(2,1)} %get-tuple-element.44), channel_id=1, source_target_pairs={{0,1},{1,2},{2,3},{3,4},{4,5},{5,6},{6,7},{8,9},{9,10},{10,11},{11... | collective-permute-start | bytes 3096584 | tf_op jit(solution)/shard_map/ppermute | solution.py:54
  81.7 16.1 %collective-permute-start.7 = (bf16[7,1,48,1536]{3,2,0,1:T(8,128)(2,1)}, bf16[7,1,48,1536]{3,2,0,1:T(8,128)(2,1)}, u32[]{:S(2)}, u32[]{:S(2)}) collective-permute-start(bf16[7,1,48,1536]{3,2,0,1:T(8,128)(2,1)} %get-tuple-element.45), channel_id=1, source_target_pairs={{1,0},{2,1},{3,2},{4,3},{5,4},{6,5},{7,6},{9,8},{10,9},{11,10},{12... | collective-permute-start | bytes 3096584 | tf_op jit(solution)/shard_map/ppermute | solution.py:56
  136.9 27.8 %slice-start = ((s8[9633792]{0:T(1024)(128)(4,1)}), s8[4194304]{0:T(1024)(128)(4,1)S(1)}, s32[]{:S(2)}) async-start(s8[9633792]{0:T(1024)(128)(4,1)} %bitcast.70), calls=%async_computation | async-start | bytes 8388608
  136.9 27.8 %slice-start.1 = ((s8[9633792]{0:T(1024)(128)(4,1)}), s8[4194304]{0:T(1024)(128)(4,1)S(1)}, s32[]{:S(2)}) async-start(s8[9633792]{0:T(1024)(128)(4,1)} %bitcast.70), calls=%async_computation.1 | async-start | bytes 8388608
  136.9 27.8 %slice-start.2 = ((s8[9633792]{0:T(1024)(128)(4,1)}), s8[1245184]{0:T(1024)(128)(4,1)S(1)}, s32[]{:S(2)}) async-start(s8[9633792]{0:T(1024)(128)(4,1)} %bitcast.70), calls=%async_computation.2 | async-start | bytes 2490368
  141.4 4.3 %copy-start = (f32[1,128]{1,0:T(1,128)S(1)}, f32[1,128]{1,0:T(1,128)}, u32[]{:S(2)}) copy-start(f32[1,128]{1,0:T(1,128)} %get-tuple-element.36) | copy-start | bytes 1540
  141.6 82.8 %collective-permute-start.8 = (bf16[7,1,48,1536]{3,2,0,1:T(8,128)(2,1)S(1)}, bf16[7,1,48,1536]{3,2,0,1:T(8,128)(2,1)S(1)}, u32[]{:S(2)}, u32[]{:S(2)}) collective-permute-start(bf16[7,1,48,1536]{3,2,0,1:T(8,128)(2,1)S(1)} %get-tuple-element.38), channel_id=1, source_target_pairs={{1,0},{2,1},{3,2},{4,3},{5,4},{6,5},{7,6},{9,8},{10,9},{11,10},{12... | collective-permute-start | bytes 3096584 | tf_op jit(solution)/shard_map/ppermute | solution.py:20
  145.7 20.1 %collective-permute-start.21 = (f32[12]{0:T(128)S(1)}, f32[12]{0:T(128)S(1)}, u32[]{:S(2)}, u32[]{:S(2)}) collective-permute-start(f32[12]{0:T(128)S(1)} %slice_bitcast_fusion.7), channel_id=1, source_target_pairs={{0,6},{1,7},{2,0},{3,1},{4,2},{5,3},{6,4},{7,5},{8,14},{9,15},{10,... | collective-permute-start | bytes 152 | tf_op jit(solution)/shard_map/ppermute | solution.py:39
  147.7 20.1 %collective-permute-start.20 = (f32[12]{0:T(128)S(1)}, f32[12]{0:T(128)S(1)}, u32[]{:S(2)}, u32[]{:S(2)}) collective-permute-start(f32[12]{0:T(128)S(1)} %slice_bitcast_fusion.7), channel_id=1, source_target_pairs={{0,5},{1,6},{2,7},{3,0},{4,1},{5,2},{6,3},{7,4},{8,13},{9,14},{10,... | collective-permute-start | bytes 152 | tf_op jit(solution)/shard_map/ppermute | solution.py:39
  156.5 13.2 %collective-permute-start.19 = (f32[12]{0:T(128)S(1)}, f32[12]{0:T(128)S(1)}, u32[]{:S(2)}, u32[]{:S(2)}) collective-permute-start(f32[12]{0:T(128)S(1)} %slice_bitcast_fusion.7), channel_id=1, source_target_pairs={{0,4},{1,5},{2,6},{3,7},{4,0},{5,1},{6,2},{7,3},{8,12},{9,13},{10,... | collective-permute-start | bytes 152 | tf_op jit(solution)/shard_map/ppermute | solution.py:39
  160.5 11.7 %collective-permute-start.18 = (f32[12]{0:T(128)S(1)}, f32[12]{0:T(128)S(1)}, u32[]{:S(2)}, u32[]{:S(2)}) collective-permute-start(f32[12]{0:T(128)S(1)} %slice_bitcast_fusion.7), channel_id=1, source_target_pairs={{0,3},{1,4},{2,5},{3,6},{4,7},{5,0},{6,1},{7,2},{8,11},{9,12},{10,... | collective-permute-start | bytes 152 | tf_op jit(solution)/shard_map/ppermute | solution.py:39
  165.8 8.9 %collective-permute-start.17 = (f32[12]{0:T(128)S(1)}, f32[12]{0:T(128)S(1)}, u32[]{:S(2)}, u32[]{:S(2)}) collective-permute-start(f32[12]{0:T(128)S(1)} %slice_bitcast_fusion.7), channel_id=1, source_target_pairs={{0,2},{1,3},{2,4},{3,5},{4,6},{5,7},{6,0},{7,1},{8,10},{9,11},{10,... | collective-permute-start | bytes 152 | tf_op jit(solution)/shard_map/ppermute | solution.py:39
  167.8 7.0 %collective-permute-start.22 = (f32[12]{0:T(128)S(1)}, f32[12]{0:T(128)S(1)}, u32[]{:S(2)}, u32[]{:S(2)}) collective-permute-start(f32[12]{0:T(128)S(1)} %slice_bitcast_fusion.7), channel_id=1, source_target_pairs={{0,7},{1,0},{2,1},{3,2},{4,3},{5,4},{6,5},{7,6},{8,15},{9,8},{10,9... | collective-permute-start | bytes 152 | tf_op jit(solution)/shard_map/ppermute | solution.py:39
  169.7 5.3 %collective-permute-start.16 = (f32[12]{0:T(128)S(1)}, f32[12]{0:T(128)S(1)}, u32[]{:S(2)}, u32[]{:S(2)}) collective-permute-start(f32[12]{0:T(128)S(1)} %slice_bitcast_fusion.7), channel_id=1, source_target_pairs={{0,1},{1,2},{2,3},{3,4},{4,5},{5,6},{6,7},{7,0},{8,9},{9,10},{10,1... | collective-permute-start | bytes 152 | tf_op jit(solution)/shard_map/ppermute | solution.py:39
  172.1 54.5 %collective-permute-start.9 = (bf16[7,1,48,1536]{3,2,0,1:T(8,128)(2,1)S(1)}, bf16[7,1,48,1536]{3,2,0,1:T(8,128)(2,1)S(1)}, u32[]{:S(2)}, u32[]{:S(2)}) collective-permute-start(bf16[7,1,48,1536]{3,2,0,1:T(8,128)(2,1)S(1)} %get-tuple-element.37), channel_id=1, source_target_pairs={{0,1},{1,2},{2,3},{3,4},{4,5},{5,6},{6,7},{8,9},{9,10},{10,11},{11... | collective-permute-start | bytes 3096584 | tf_op jit(solution)/shard_map/ppermute | solution.py:20
  175.0 11.1 %collective-permute-start.29 = (f32[12]{0:T(128)S(1)}, f32[12]{0:T(128)S(1)}, u32[]{:S(2)}, u32[]{:S(2)}) collective-permute-start(f32[12]{0:T(128)S(1)} %maximum_maximum_fusion.2), channel_id=1, source_target_pairs={{0,56},{8,0},{16,8},{24,16},{32,24},{40,32},{48,40},{56,48},{64,12... | collective-permute-start | bytes 152 | tf_op jit(solution)/shard_map/ppermute | solution.py:39
  176.9 11.1 %collective-permute-start.28 = (f32[12]{0:T(128)S(1)}, f32[12]{0:T(128)S(1)}, u32[]{:S(2)}, u32[]{:S(2)}) collective-permute-start(f32[12]{0:T(128)S(1)} %maximum_maximum_fusion.2), channel_id=1, source_target_pairs={{0,48},{8,56},{16,0},{24,8},{32,16},{40,24},{48,32},{56,40},{64,11... | collective-permute-start | bytes 152 | tf_op jit(solution)/shard_map/ppermute | solution.py:39
  178.8 14.0 %collective-permute-start.27 = (f32[12]{0:T(128)S(1)}, f32[12]{0:T(128)S(1)}, u32[]{:S(2)}, u32[]{:S(2)}) collective-permute-start(f32[12]{0:T(128)S(1)} %maximum_maximum_fusion.2), channel_id=1, source_target_pairs={{0,40},{8,48},{16,56},{24,0},{32,8},{40,16},{48,24},{56,32},{64,10... | collective-permute-start | bytes 152 | tf_op jit(solution)/shard_map/ppermute | solution.py:39
  186.1 11.1 %collective-permute-start.26 = (f32[12]{0:T(128)S(1)}, f32[12]{0:T(128)S(1)}, u32[]{:S(2)}, u32[]{:S(2)}) collective-permute-start(f32[12]{0:T(128)S(1)} %maximum_maximum_fusion.2), channel_id=1, source_target_pairs={{0,32},{8,40},{16,48},{24,56},{32,0},{40,8},{48,16},{56,24},{64,96... | collective-permute-start | bytes 152 | tf_op jit(solution)/shard_map/ppermute | solution.py:39
  188.0 11.1 %collective-permute-start.25 = (f32[12]{0:T(128)S(1)}, f32[12]{0:T(128)S(1)}, u32[]{:S(2)}, u32[]{:S(2)}) collective-permute-start(f32[12]{0:T(128)S(1)} %maximum_maximum_fusion.2), channel_id=1, source_target_pairs={{0,24},{8,32},{16,40},{24,48},{32,56},{40,0},{48,8},{56,16},{64,88... | collective-permute-start | bytes 152 | tf_op jit(solution)/shard_map/ppermute | solution.py:39
  192.9 7.9 %collective-permute-start.24 = (f32[12]{0:T(128)S(1)}, f32[12]{0:T(128)S(1)}, u32[]{:S(2)}, u32[]{:S(2)}) collective-permute-start(f32[12]{0:T(128)S(1)} %maximum_maximum_fusion.2), channel_id=1, source_target_pairs={{0,16},{8,24},{16,32},{24,40},{32,48},{40,56},{48,0},{56,8},{64,80... | collective-permute-start | bytes 152 | tf_op jit(solution)/shard_map/ppermute | solution.py:39
  197.2 7.6 %collective-permute-start.23 = (f32[12]{0:T(128)S(1)}, f32[12]{0:T(128)S(1)}, u32[]{:S(2)}, u32[]{:S(2)}) collective-permute-start(f32[12]{0:T(128)S(1)} %maximum_maximum_fusion.2), channel_id=1, source_target_pairs={{0,8},{8,16},{16,24},{24,32},{32,40},{40,48},{48,56},{56,0},{64,72... | collective-permute-start | bytes 152 | tf_op jit(solution)/shard_map/ppermute | solution.py:39
  204.8 24.0 %collective-permute-start.36 = (f32[12]{0:T(128)S(1)}, f32[12]{0:T(128)S(1)}, u32[]{:S(2)}, u32[]{:S(2)}) collective-permute-start(f32[12]{0:T(128)S(1)} %maximum_maximum_fusion.1), channel_id=1, source_target_pairs={{0,448},{8,456},{16,464},{24,472},{32,480},{40,488},{48,496},{56,5... | collective-permute-start | bytes 152 | tf_op jit(solution)/shard_map/ppermute | solution.py:39
  206.7 30.6 %collective-permute-start.35 = (f32[12]{0:T(128)S(1)}, f32[12]{0:T(128)S(1)}, u32[]{:S(2)}, u32[]{:S(2)}) collective-permute-start(f32[12]{0:T(128)S(1)} %maximum_maximum_fusion.1), channel_id=1, source_target_pairs={{0,384},{8,392},{16,400},{24,408},{32,416},{40,424},{48,432},{56,4... | collective-permute-start | bytes 152 | tf_op jit(solution)/shard_map/ppermute | solution.py:39
  213.8 32.1 %collective-permute-start.34 = (f32[12]{0:T(128)S(1)}, f32[12]{0:T(128)S(1)}, u32[]{:S(2)}, u32[]{:S(2)}) collective-permute-start(f32[12]{0:T(128)S(1)} %maximum_maximum_fusion.1), channel_id=1, source_target_pairs={{0,320},{8,328},{16,336},{24,344},{32,352},{40,360},{48,368},{56,3... | collective-permute-start | bytes 152 | tf_op jit(solution)/shard_map/ppermute | solution.py:39
  224.4 25.3 %collective-permute-start.33 = (f32[12]{0:T(128)S(1)}, f32[12]{0:T(128)S(1)}, u32[]{:S(2)}, u32[]{:S(2)}) collective-permute-start(f32[12]{0:T(128)S(1)} %maximum_maximum_fusion.1), channel_id=1, source_target_pairs={{0,256},{8,264},{16,272},{24,280},{32,288},{40,296},{48,304},{56,3... | collective-permute-start | bytes 152 | tf_op jit(solution)/shard_map/ppermute | solution.py:39
  228.1 38.3 %collective-permute-start.10 = (bf16[1,128,1536]{2,1,0:T(8,128)(2,1)S(1)}, bf16[1,128,1536]{2,1,0:T(8,128)(2,1)S(1)}, u32[]{:S(2)}, u32[]{:S(2)}) collective-permute-start(bf16[1,128,1536]{2,1,0:T(8,128)(2,1)S(1)} %get-tuple-element.39), channel_id=1, source_target_pairs={{384,0},{392,8},{400,16},{408,24},{416,32},{424,40},{432,48},{440,... | collective-permute-start | bytes 1179656 | tf_op jit(solution)/shard_map/ppermute | solution.py:20
  228.8 22.2 %collective-permute-start.32 = (f32[12]{0:T(128)S(1)}, f32[12]{0:T(128)S(1)}, u32[]{:S(2)}, u32[]{:S(2)}) collective-permute-start(f32[12]{0:T(128)S(1)} %maximum_maximum_fusion.1), channel_id=1, source_target_pairs={{0,192},{8,200},{16,208},{24,216},{32,224},{40,232},{48,240},{56,2... | collective-permute-start | bytes 152 | tf_op jit(solution)/shard_map/ppermute | solution.py:39
  237.3 18.7 %collective-permute-start.31 = (f32[12]{0:T(128)S(1)}, f32[12]{0:T(128)S(1)}, u32[]{:S(2)}, u32[]{:S(2)}) collective-permute-start(f32[12]{0:T(128)S(1)} %maximum_maximum_fusion.1), channel_id=1, source_target_pairs={{0,128},{8,136},{16,144},{24,152},{32,160},{40,168},{48,176},{56,1... | collective-permute-start | bytes 152 | tf_op jit(solution)/shard_map/ppermute | solution.py:39
  245.9 19.1 %collective-permute-start.30 = (f32[12]{0:T(128)S(1)}, f32[12]{0:T(128)S(1)}, u32[]{:S(2)}, u32[]{:S(2)}) collective-permute-start(f32[12]{0:T(128)S(1)} %maximum_maximum_fusion.1), channel_id=1, source_target_pairs={{0,64},{8,72},{16,80},{24,88},{32,96},{40,104},{48,112},{56,120},{... | collective-permute-start | bytes 152 | tf_op jit(solution)/shard_map/ppermute | solution.py:39
  249.7 17.8 %collective-permute-start.14 = (bf16[1,128,1536]{2,1,0:T(8,128)(2,1)S(1)}, bf16[1,128,1536]{2,1,0:T(8,128)(2,1)S(1)}, u32[]{:S(2)}, u32[]{:S(2)}) collective-permute-start(bf16[1,128,1536]{2,1,0:T(8,128)(2,1)S(1)} %get-tuple-element.40), channel_id=1, source_target_pairs={{0,256},{8,264},{16,272},{24,280},{32,288},{40,296},{48,304},{56,3... | collective-permute-start | bytes 1179656 | tf_op jit(solution)/shard_map/ppermute | solution.py:20
  251.0 17.0 %collective-permute-start.13 = (bf16[1,128,1536]{2,1,0:T(8,128)(2,1)S(1)}, bf16[1,128,1536]{2,1,0:T(8,128)(2,1)S(1)}, u32[]{:S(2)}, u32[]{:S(2)}) collective-permute-start(bf16[1,128,1536]{2,1,0:T(8,128)(2,1)S(1)} %get-tuple-element.41), channel_id=1, source_target_pairs={{0,128},{8,136},{16,144},{24,152},{32,160},{40,168},{48,176},{56,1... | collective-permute-start | bytes 1179656 | tf_op jit(solution)/shard_map/ppermute | solution.py:20
  256.0 43.8 %collective-permute-start.12 = (bf16[1,128,1536]{2,1,0:T(8,128)(2,1)S(1)}, bf16[1,128,1536]{2,1,0:T(8,128)(2,1)S(1)}, u32[]{:S(2)}, u32[]{:S(2)}) collective-permute-start(bf16[1,128,1536]{2,1,0:T(8,128)(2,1)S(1)} %get-tuple-element.42), channel_id=1, source_target_pairs={{128,0},{136,8},{144,16},{152,24},{160,32},{168,40},{176,48},{184,... | collective-permute-start | bytes 1179656 | tf_op jit(solution)/shard_map/ppermute | solution.py:20
  265.0 40.7 %collective-permute-start.11 = (bf16[1,128,1536]{2,1,0:T(8,128)(2,1)S(1)}, bf16[1,128,1536]{2,1,0:T(8,128)(2,1)S(1)}, u32[]{:S(2)}, u32[]{:S(2)}) collective-permute-start(bf16[1,128,1536]{2,1,0:T(8,128)(2,1)S(1)} %get-tuple-element.43), channel_id=1, source_target_pairs={{256,0},{264,8},{272,16},{280,24},{288,32},{296,40},{304,48},{312,... | collective-permute-start | bytes 1179656 | tf_op jit(solution)/shard_map/ppermute | solution.py:20
  266.3 39.4 %collective-permute-start.15 = (bf16[1,128,1536]{2,1,0:T(8,128)(2,1)S(1)}, bf16[1,128,1536]{2,1,0:T(8,128)(2,1)S(1)}, u32[]{:S(2)}, u32[]{:S(2)}) collective-permute-start(bf16[1,128,1536]{2,1,0:T(8,128)(2,1)S(1)} %slice_bitcast_fusion.1), channel_id=1, source_target_pairs={{0,384},{8,392},{16,400},{24,408},{32,416},{40,424},{48,432},{56,4... | collective-permute-start | bytes 1179656 | tf_op jit(solution)/shard_map/ppermute | solution.py:20
